TPU v7x, 256 devices: a whole 4x4x8 slice. The times are simulated.
256 devices in a mesh: req: 32 (over x, y, core), tp: 8 (over z).
Axes of the slice: x: 4, y: 4, z: 8, core: 2. Of those that a mesh axis runs over, the one named last changes fastest.
Arguments:
- query: bfloat16 [768, 4096], P('req', 'tp'), may hold values from -102 to 102
- new_key: bfloat16 [768, 1024], P('req', 'tp'), may hold values from -6 to 6
- new_value: bfloat16 [768, 1024], P('req', 'tp'), may hold values from -6 to 6
- prefix_key: bfloat16 [64, 6144, 1024], P('req', None, 'tp'), may hold values from -6 to 6
- prefix_value: bfloat16 [64, 6144, 1024], P('req', None, 'tp'), may hold values from -6 to 6
- suffix_key: bfloat16 [768, 128, 1024], P('req', None, 'tp'), may hold values from -6 to 6
- suffix_value: bfloat16 [768, 128, 1024], P('req', None, 'tp'), may hold values from -6 to 6
- group_ids: int32 [768], replicated, may hold values from 0 to 63, as said below
- prompt_len: int32 [64], P('req'), may hold values from 768 to 6144, as said below
- suffix_len: int32 [768], replicated, may hold values from 1 to 128, as said below
- o_weight: bfloat16 [4096, 4096], P('tp'), may hold values from -0.09375 to 0.09375
- residual: bfloat16 [768, 4096], P('req'), may hold values from -0.29882812 to 0.29882812
- norm_gain: bfloat16 [4096], replicated, may hold values from 0.5 to 1.5
Outputs:
- hidden: bfloat16 [768, 4096], P('req')
- normed: bfloat16 [768, 4096], P('req')
Inputs may be any that keep to these rules, and one draw needn't show every extreme that they name: Request r belongs to group group_ids[r]; groups 2k to 2k + 1 at a time are held together (group // 2 names the holder). Among each aligned block of 24 requests, every holder that appears is named by exactly 2 of them. `prompt_len`: some group has exactly 6144. `suffix_len`: some request has exactly 128.
All inputs are finite; a program needn't handle non-finite values.
Results may differ from a plain program's by a relative error of at most 0.008.
Values may be sent and summed in bfloat16 or wider, within the bound.
No kernel may reach another device: no remote copies, remote signals or barrier semaphores. Data moves between devices by JAX's collectives and lax.ppermute only.
A program may use at most 64 MiB of HBM per device.

v0:
```python
import math
import jax
import jax.numpy as jnp
from jax import lax
from jax.sharding import PartitionSpec as P

HD = 128
WIN = 4096
SINKS = 4
FAR_BELOW = -1e30
NORM_EPS = 1e-06


def prefix_attend(
    rows_query, row_group, row_suffix, prefix_key, prefix_value, prompt_len, first_group, blocks
):
    row_count = rows_query.shape[0]
    groups_dev = prefix_key.shape[0]
    prompt_max = prefix_key.shape[1]
    kv_dev = prefix_key.shape[2] // HD
    heads_dev = rows_query.shape[1] // HD
    repeat = heads_dev // kv_dev
    block_len = min(512, prompt_max)
    score_scale = 1.0 / math.sqrt(HD)
    local_group = row_group - first_group
    owned = (local_group >= 0) & (local_group < groups_dev)
    member = local_group[:, None] == jnp.arange(groups_dev, dtype=jnp.int32)[None, :]
    row_prompt = jnp.sum(jnp.where(member, prompt_len[None, :], 0), axis=1)
    row_low = row_prompt + row_suffix - WIN + 1
    queries = rows_query.reshape(row_count, kv_dev, repeat, HD)

    def key_step(block_index, loop_state):
        running, weight_sum, weighted = loop_state
        key_start = block_index * block_len
        key_block = lax.dynamic_slice_in_dim(prefix_key, key_start, block_len, 1).reshape(
            groups_dev, block_len, kv_dev, HD
        )
        value_block = lax.dynamic_slice_in_dim(prefix_value, key_start, block_len, 1).reshape(
            groups_dev, block_len, kv_dev, HD
        )
        scores = (
            jnp.einsum("rkhd,gpkd->rkhgp", queries, key_block, preferred_element_type=jnp.float32)
            * score_scale
        )
        positions = key_start + jnp.arange(block_len, dtype=jnp.int32)
        inside = positions[None, :] < prompt_len[:, None]
        window = (positions[None, :] < SINKS) | (positions[None, :] >= row_low[:, None])
        usable = member[:, :, None] & inside[None, :, :] & window[:, None, :]
        usable = usable[:, None, None, :, :]
        masked = jnp.where(usable, scores, FAR_BELOW)
        updated = jnp.maximum(running, jnp.max(masked, axis=(3, 4)))
        weights = jnp.where(usable, jnp.exp(masked - updated[..., None, None]), 0.0)
        rescale = jnp.exp(running - updated)
        weight_sum = weight_sum * rescale + jnp.sum(weights, axis=(3, 4))
        rounded = weights.astype(jnp.bfloat16)
        weighted = weighted * rescale[..., None] + jnp.einsum(
            "rkhgp,gpkd->rkhd", rounded, value_block, preferred_element_type=jnp.float32
        )
        return (updated, weight_sum, weighted)

    initial = (
        jnp.full((row_count, kv_dev, repeat), FAR_BELOW, jnp.float32),
        jnp.zeros((row_count, kv_dev, repeat), jnp.float32),
        jnp.zeros((row_count, kv_dev, repeat, HD), jnp.float32),
    )
    running, weight_sum, weighted = lax.fori_loop(0, blocks, key_step, initial)
    bounded = jnp.maximum(weight_sum, 1.0)
    normalized = jnp.where(owned[:, None, None, None], weighted / bounded[..., None], 0.0).reshape(
        row_count, heads_dev * HD
    )
    log_total = jnp.where(owned[:, None, None], running + jnp.log(bounded), 0.0).reshape(
        row_count, heads_dev
    )
    return (normalized, log_total)


def body(
    query,
    new_key,
    new_value,
    prefix_key,
    prefix_value,
    suffix_key,
    suffix_value,
    group_ids,
    prompt_len,
    suffix_len,
    o_weight,
    residual,
    norm_gain,
):
    req_dev = query.shape[0]
    heads_dev = query.shape[1] // HD
    kv_dev = new_key.shape[1] // HD
    repeat = heads_dev // kv_dev
    groups_dev = prefix_key.shape[0]
    prompt_max = prefix_key.shape[1]
    suffix_max = suffix_key.shape[1]
    block_len = min(512, prompt_max)
    score_scale = 1.0 / math.sqrt(HD)
    places = lax.axis_size("req")
    device = lax.axis_index("req")
    first_group = device * groups_dev
    own_suffix = lax.dynamic_slice_in_dim(suffix_len, device * req_dev, req_dev)
    blocks = prompt_max // block_len
    capacity = max(2, req_dev // places)
    slot_total = places * capacity
    all_groups = group_ids.reshape(places, 1, req_dev)
    all_suffix = suffix_len.reshape(places, 1, req_dev)
    all_rows = (
        jnp.arange(places, dtype=jnp.int32)[:, None] * req_dev
        + jnp.arange(req_dev, dtype=jnp.int32)[None, :]
    ).reshape(places, 1, req_dev)
    is_mine = (group_ids // groups_dev).reshape(places, req_dev) == device
    slot_order = jnp.cumsum(is_mine.astype(jnp.int32), axis=1) - 1
    slot_pick = is_mine[:, None, :] & (
        slot_order[:, None, :] == jnp.arange(capacity, dtype=jnp.int32)[None, :, None]
    )
    filled = jnp.any(slot_pick, axis=2)
    slot_group = jnp.where(
        filled, jnp.sum(jnp.where(slot_pick, all_groups, 0), axis=2), -1
    ).reshape(slot_total)
    slot_suffix = jnp.sum(jnp.where(slot_pick, all_suffix, 0), axis=2).reshape(slot_total)
    slot_row = jnp.where(filled, jnp.sum(jnp.where(slot_pick, all_rows, 0), axis=2), -1).reshape(
        slot_total
    )
    every_query = lax.all_gather(query, "req", axis=0, tiled=True)
    pick_rows = slot_row[:, None] == jnp.arange(places * req_dev, dtype=jnp.int32)[None, :]
    compact = jnp.dot(
        pick_rows.astype(jnp.bfloat16), every_query, preferred_element_type=jnp.float32
    ).astype(jnp.bfloat16)
    part_out, part_log = prefix_attend(
        compact, slot_group, slot_suffix, prefix_key, prefix_value, prompt_len, first_group, blocks
    )
    spread_rows = pick_rows.T.astype(jnp.float32)
    spread_out = jnp.dot(spread_rows, part_out, precision=lax.Precision.HIGHEST)
    spread_log = jnp.dot(spread_rows, part_log, precision=lax.Precision.HIGHEST)
    prefix_out, prefix_log = (
        lax.psum_scatter(spread_out, "req", scatter_dimension=0, tiled=True),
        lax.psum_scatter(spread_log, "req", scatter_dimension=0, tiled=True),
    )
    queries = query.reshape(req_dev, kv_dev, repeat, HD)
    key_rows = suffix_key.reshape(req_dev, suffix_max, kv_dev, HD)
    value_rows = suffix_value.reshape(req_dev, suffix_max, kv_dev, HD)
    scores = (
        jnp.einsum("rkhd,rjkd->rkhj", queries, key_rows, preferred_element_type=jnp.float32)
        * score_scale
    )
    own_score = (
        jnp.einsum(
            "rkhd,rkd->rkh",
            queries,
            new_key.reshape(req_dev, kv_dev, HD),
            preferred_element_type=jnp.float32,
        )
        * score_scale
    )
    usable = (jnp.arange(suffix_max, dtype=jnp.int32)[None, :] < own_suffix[:, None])[
        :, None, None, :
    ]
    masked = jnp.where(usable, scores, FAR_BELOW)
    running = jnp.maximum(jnp.max(masked, axis=-1), own_score)
    weights = jnp.where(usable, jnp.exp(masked - running[..., None]), 0.0)
    own_weight = jnp.exp(own_score - running)
    weight_sum = jnp.sum(weights, axis=-1) + own_weight
    weighted = jnp.einsum(
        "rkhj,rjkd->rkhd",
        weights.astype(jnp.bfloat16),
        value_rows,
        preferred_element_type=jnp.float32,
    )
    own_rounded = own_weight.astype(jnp.bfloat16).astype(jnp.float32)
    weighted = weighted + own_rounded[..., None] * new_value.reshape(req_dev, kv_dev, 1, HD).astype(
        jnp.float32
    )
    local_out = weighted / weight_sum[..., None]
    local_log = running + jnp.log(weight_sum)
    prefix_out = prefix_out.reshape(req_dev, kv_dev, repeat, HD)
    prefix_log = prefix_log.reshape(req_dev, kv_dev, repeat)
    combined = jnp.logaddexp(prefix_log, local_log)
    attended = (
        prefix_out * jnp.exp(prefix_log - combined)[..., None]
        + local_out * jnp.exp(local_log - combined)[..., None]
    )
    attended = attended.reshape(req_dev, heads_dev * HD).astype(jnp.bfloat16)
    partial_value = jnp.dot(attended, o_weight, preferred_element_type=jnp.float32)
    proj = lax.psum(partial_value, "tp")
    summed = residual.astype(jnp.float32) + proj
    hidden = summed.astype(jnp.bfloat16)
    inverse = lax.rsqrt(jnp.mean(summed * summed, axis=-1, keepdims=True) + NORM_EPS)
    normed = (summed * inverse * norm_gain.astype(jnp.float32)[None, :]).astype(jnp.bfloat16)
    return (hidden, normed)


def solution(mesh):
    placed = (
        P("req", "tp"),
        P("req", "tp"),
        P("req", "tp"),
        P("req", None, "tp"),
        P("req", None, "tp"),
        P("req", None, "tp"),
        P("req", None, "tp"),
        P(),
        P("req"),
        P(),
        P("tp", None),
        P("req", None),
        P(),
    )
    return jax.shard_map(
        body,
        mesh=mesh,
        in_specs=placed,
        out_specs=(P("req", None), P("req", None)),
        check_vma=False,
    )
```

profile of v0, /device:TPU:2, one launch (start us, length us, event | category | flops | bytes accessed | tf_op | source)
XLA Modules:
  0.0 305.6 jit_solution(10688126659396240701)
XLA Ops:
  7.3 0.8 fusion.51
  8.2 0.8 broadcast_in_dim.180
  9.3 0.8 broadcast_in_dim.188
  10.5 0.7 fusion.59
  11.4 24.9 %all_gather.3 = bf16[768,512]{1,0:T(8,128)(2,1)S(1)} all-gather(bf16[24,512]{1,0:T(8,128)(2,1)} %param.15), channel_id=1, replica_groups=mesh['req'=32,'tp'=8] {'req'}, dimensions={0}, use_global_device_ids=true | all-gather | bytes 811008 | tf_op jit(solution)/shard_map/all_gather | solution.py:127
  36.8 50.0 %while.18 = (s32[]{:T(128)}, f32[64,1,4]{0,2,1:T(4,128)S(1)}, f32[64,1,4]{0,2,1:T(4,128)S(1)}, f32[64,1,4,128]{3,0,2,1:T(8,128)S(1)}, s32[2]{0:T(128)}, /*index=...) while((s32[]{:T(128)}, f32[64,1,4]{0,2,1:T(4,128)S(1)}, ...), condition=%wide.region_9.10_spmd.clone, body=%wide.region_6.9_spmd.clone.sunk | while | flops 136876160 | bytes 4351967 | solution.py:66
  37.0 0.7 broadcast_compare_fusion.5
  37.8 1.4 fusion.83
  39.6 1.4 fusion.86
  41.2 0.7 broadcast_compare_fusion.5
  42.0 1.4 fusion.83
  43.8 1.4 fusion.86
  45.3 0.7 broadcast_compare_fusion.5
  46.2 1.4 fusion.83
  47.9 1.4 fusion.86
  49.5 0.7 broadcast_compare_fusion.5
  50.3 1.4 fusion.83
  52.1 1.4 fusion.86
  53.7 0.7 broadcast_compare_fusion.5
  54.5 1.4 fusion.83
  56.3 1.4 fusion.86
  57.8 0.7 broadcast_compare_fusion.5
  58.7 1.4 fusion.83
  60.5 1.4 fusion.86
  62.0 0.7 broadcast_compare_fusion.5
  62.9 1.4 fusion.83
  64.6 1.4 fusion.86
  66.2 0.7 broadcast_compare_fusion.5
  67.0 1.4 fusion.83
  68.8 1.4 fusion.86
  70.3 0.7 broadcast_compare_fusion.5
  71.2 1.4 fusion.83
  73.0 1.4 fusion.86
  75.4 1.4 fusion.83
  77.1 1.4 fusion.86
  78.7 0.7 broadcast_compare_fusion.5
  79.5 1.4 fusion.83
  81.3 1.4 fusion.86
  83.7 1.4 fusion.83
  85.5 1.4 fusion.86
  87.2 2.0 fusion.27
  89.3 0.8 dynamic_slice.17
  91.6 109.0 %all-reduce = f32[768,4]{0,1:T(4,128)S(1)} all-reduce(f32[768,4]{0,1:T(4,128)S(1)} %fusion.26), channel_id=3, replica_groups=mesh['req'=32,'tp'=8] {'req'}, use_global_device_ids=true, to_apply=%region_11.12.clone | all-reduce | flops 3072 | bytes 24576
  201.9 0.8 reshape.377
  203.2 3.6 %fusion.37 = f32[24,4096]{1,0:T(8,128)} fusion(bf16[512,4096]{1,0:T(8,128)(2,1)} %param.25, bf16[3,8,4,128]{3,2,1,0:T(4,128)(2,1)S(1)} %bitcast.93), kind=kOutput, calls=%fused_computation.57 | convolution fusion | flops 100663296 | bytes 4612096 | tf_op jit(solution)/shard_map/dot_general | solution.py:186
  206.8 88.9 %all-reduce.3.cloned.1.call-done = f32[24,4096]{1,0:T(8,128)} async-done(((f32[24,4096]{1,0:T(8,128)}), f32[24,4096]{1,0:T(8,128)}) %all-reduce.3.cloned.1.call-update) | async-done | bytes 393232 | tf_op jit(solution)/shard_map/psum | solution.py:187
  295.8 1.2 multiply_reduce_fusion
  297.0 1.8 multiply_convert_fusion
  (177 shorter events, 13.2 us)
Async XLA Ops:
  7.2 193.8 %copy-start = (bf16[24,128,128]{2,1,0:T(8,128)(2,1)S(1)}, bf16[24,128,128]{2,1,0:T(8,128)(2,1)}, u32[]{:S(2)}) copy-start(bf16[24,128,128]{2,1,0:T(8,128)(2,1)} %param.20) | copy-start | bytes 2359300
  7.2 194.8 %reduce-scatter.3.cloned.1.call-start = ((), (), s32[]{:S(2)}) async-start(), calls=%async_computation.1 | async-start | bytes 1622016 | tf_op jit(solution)/shard_map/reduce_scatter | solution.py:139
  86.9 2.4 copy-start.2
  86.9 3.2 %copy-start.7 = (u32[256]{0:T(256)S(1)}, u32[256]{0:T(256)}, u32[]{:S(2)}) copy-start(u32[256]{0:T(256)} %constant.130) | copy-start | bytes 3076
  86.9 113.9 %copy-start.4 = (bf16[24,128]{1,0:T(8,128)(2,1)S(1)}, bf16[24,128]{1,0:T(8,128)(2,1)}, u32[]{:S(2)}) copy-start(bf16[24,128]{1,0:T(8,128)(2,1)} %param.17) | copy-start | bytes 18436
  86.9 113.9 %copy-start.6 = (bf16[24,128]{1,0:T(8,128)(2,1)S(1)}, bf16[24,128]{1,0:T(8,128)(2,1)}, u32[]{:S(2)}) copy-start(bf16[24,128]{1,0:T(8,128)(2,1)} %param.16) | copy-start | bytes 18436
  86.9 115.8 %copy-start.5 = (bf16[24,128,128]{2,1,0:T(8,128)(2,1)S(1)}, bf16[24,128,128]{2,1,0:T(8,128)(2,1)}, u32[]{:S(2)}) copy-start(bf16[24,128,128]{2,1,0:T(8,128)(2,1)} %param.21) | copy-start | bytes 2359300
  89.2 206.5 %all-reduce.3.cloned.1.call-start = ((), (), s32[]{:S(2)}) async-start(), calls=%async_computation.2 | async-start | bytes 786432 | tf_op jit(solution)/shard_map/psum | solution.py:187
  202.8 4.0 %copy-start.3 = (bf16[4096]{0:T(1024)(128)(2,1)S(1)}, bf16[4096]{0:T(1024)(128)(2,1)}, u32[]{:S(2)}) copy-start(bf16[4096]{0:T(1024)(128)(2,1)} %param.27) | copy-start | bytes 24580
  202.8 93.0 %copy-start.1 = (bf16[24,4096]{1,0:T(8,128)(2,1)S(1)}, bf16[24,4096]{1,0:T(8,128)(2,1)}, u32[]{:S(2)}) copy-start(bf16[24,4096]{1,0:T(8,128)(2,1)} %param.26) | copy-start | bytes 589828
Sparse Core Ops, SparseCore 0:
  89.4 86.8 reduce-scatter.2
  206.9 88.8 all-reduce.2
where the time goes:
time: 307 us; the launch traced here: 306 us
  blocking collectives  134 us (44%)
  waiting for transfers between devices  89 us (29%)
  matrix products  40.4 us (13%)
  other arithmetic  21.3 us (7%)
  between operations  15 us (5%)
  local copies, waits for them, and re-layouts  5.04 us (2%)
    unnamed x1, blocking collectives  109 us
    psum x1, waiting for transfers between devices, body(): proj = lax.psum(partial_value, 'tp')  88.9 us
    all_gather x1, blocking collectives, body(): every_query = lax.all_gather(query, 'req', axis=0, tiled=True)  24.9 us
    dot_general x12, matrix products, key_step(): jnp.einsum('rkhgp,gpkd->rkhd', rounded, value_block, preferred_element_ty...  16.8 us
    dot_general x12, matrix products, key_step(): jnp.einsum('rkhd,gpkd->rkhgp', queries, key_block, preferred_element_type...  16.3 us
    lt x12, other arithmetic, key_step(): inside = positions[None, :] < prompt_len[:, None]  8.77 us
  transfers between devices with their start and end apart: 2, of which 1 were waited for; matrix products, arithmetic and copies ran while one was open for 1% of the time, Pallas kernels for 0%

commit v1 on v0

--- a/solution.py
+++ b/solution.py
@@ -124,7 +124,11 @@
     slot_row = jnp.where(filled, jnp.sum(jnp.where(slot_pick, all_rows, 0), axis=2), -1).reshape(
         slot_total
     )
-    every_query = lax.all_gather(query, "req", axis=0, tiled=True)
+    size = lax.axis_size("req")
+    repeats = [size if d == 0 else 1 for d in range(query.ndim)]
+    every_query = lax.all_to_all(
+        jnp.tile(query, repeats), "req", split_axis=0, concat_axis=0, tiled=True
+    )
     pick_rows = slot_row[:, None] == jnp.arange(places * req_dev, dtype=jnp.int32)[None, :]
     compact = jnp.dot(
         pick_rows.astype(jnp.bfloat16), every_query, preferred_element_type=jnp.float32

time: 307 us -> 292 us (0.951)
  blocking collectives: 134 us -> 110 us
  other arithmetic: 21.3 us -> 13.3 us
  waiting for transfers between devices: 89 us -> 96.8 us
  starting transfers between devices: 0.08 us -> 7.7 us
    all_gather x1 -> x0, blocking collectives: 24.9 us -> none  [body(): every_query = lax.all_gather(query, 'req', axis=0, tiled=True)]
    lt x12, other arithmetic: 8.77 us -> 0.89 us  [key_step(): inside = positions[None, :] < prompt_len[:, None]]
    all_to_all x0 -> x1, waiting for transfers between devices: none -> 7.68 us  [body(): lax.all_to_all(jnp.tile(query, repeats), 'req', split_axis=0, concat_axis...]
    all_to_all x0 -> x1, starting transfers between devices: none -> 7.62 us  [body(): lax.all_to_all(jnp.tile(query, repeats), 'req', split_axis=0, concat_axis...]
  transfers between devices with their start and end apart: 2 -> 3, of which waited for: 1 -> 2; matrix products, arithmetic and copies ran while one was open for 1% -> 2% of each run, Pallas kernels for 0% -> 0%
where the time goes in v1:
time: 292 us; the launch traced here: 291 us
  blocking collectives  110 us (38%)
  waiting for transfers between devices  96.8 us (33%)
  matrix products  40.4 us (14%)
  between operations  15 us (5%)
  other arithmetic  13.3 us (5%)
  starting transfers between devices  7.7 us (3%)
  local copies, waits for them, and re-layouts  6.8 us (2%)
    unnamed x1, blocking collectives  110 us
    psum x1, waiting for transfers between devices, body(): proj = lax.psum(partial_value, 'tp')  89.1 us
    dot_general x12, matrix products, key_step(): jnp.einsum('rkhgp,gpkd->rkhd', rounded, value_block, preferred_element_ty...  16.8 us
    dot_general x12, matrix products, key_step(): jnp.einsum('rkhd,gpkd->rkhgp', queries, key_block, preferred_element_type...  16.3 us
    all_to_all x1, waiting for transfers between devices, body(): lax.all_to_all(jnp.tile(query, repeats), 'req', split_axis=0, concat_axis...  7.68 us
    all_to_all x1, starting transfers between devices, body(): lax.all_to_all(jnp.tile(query, repeats), 'req', split_axis=0, concat_axis...  7.62 us
  transfers between devices with their start and end apart: 3, of which 2 were waited for; matrix products, arithmetic and copies ran while one was open for 2% of the time, Pallas kernels for 0%

profile of v1, /device:TPU:2, one launch (start us, length us, event | category | flops | bytes accessed | tf_op | source)
XLA Modules:
  0.0 290.8 jit_solution(12943070124509745079)
XLA Ops:
  7.2 1.7 tile.2
  8.9 7.6 %all-to-all-start = ((bf16[32,24,512]{2,1,0:T(8,128)(2,1)}), bf16[32,24,512]{2,1,0:T(8,128)(2,1)S(1)}, u32[]{:S(2)}, u32[]{:S(2)}) async-start(bf16[32,24,512]{2,1,0:T(8,128)(2,1)} %tile.2), calls=%async_computation | async-start | bytes 1572864 | tf_op jit(solution)/shard_map/all_to_all | solution.py:129
  16.6 0.7 fusion.51
  17.5 0.8 broadcast_in_dim.180
  18.6 0.8 broadcast_in_dim.188
  20.2 0.7 fusion.59
  20.9 7.7 %all-to-all-done = bf16[32,24,512]{2,1,0:T(8,128)(2,1)S(1)} async-done(((bf16[32,24,512]{2,1,0:T(8,128)(2,1)}), bf16[32,24,512]{2,1,0:T(8,128)(2,1)S(1)}, u32[]{:S(2)}, u32[]{:S(2)}) %all-to-all-start) | async-done | bytes 786464 | tf_op jit(solution)/shard_map/all_to_all | solution.py:129
  29.0 42.2 %while.18 = (s32[]{:T(128)}, f32[64,1,4]{0,2,1:T(4,128)S(1)}, f32[64,1,4]{0,2,1:T(4,128)S(1)}, f32[64,1,4,128]{3,0,2,1:T(8,128)S(1)}, s32[2]{0:T(128)S(1)}, /*in...) while((s32[]{:T(128)}, f32[64,1,4]{0,2,1:T(4,128)S(1)}, ...), condition=%wide.region_9.10_spmd.clone, body=%wide.region_6.9_spmd.clone.sunk | while | flops 136876160 | bytes 4351967 | solution.py:66
  29.3 1.4 fusion.83
  30.7 0.4 fusion.85
  31.1 1.4 fusion.86
  32.8 1.4 fusion.83
  34.2 0.4 fusion.85
  34.6 1.4 fusion.86
  36.3 1.4 fusion.83
  37.7 0.4 fusion.85
  38.1 1.4 fusion.86
  39.9 1.4 fusion.83
  41.2 0.4 fusion.85
  41.6 1.4 fusion.86
  43.4 1.4 fusion.83
  44.8 0.4 fusion.85
  45.1 1.4 fusion.86
  46.9 1.4 fusion.83
  48.7 1.4 fusion.86
  50.4 1.4 fusion.83
  52.2 1.4 fusion.86
  53.9 1.4 fusion.83
  55.7 1.4 fusion.86
  57.4 1.4 fusion.83
  59.2 1.4 fusion.86
  60.9 1.4 fusion.83
  62.7 1.4 fusion.86
  64.5 1.4 fusion.83
  66.2 1.4 fusion.86
  68.0 1.4 fusion.83
  69.7 1.4 fusion.86
  71.4 2.0 fusion.27
  73.6 0.8 dynamic_slice.17
  74.4 0.6 dynamic-slice
  75.8 0.6 fusion.68
  76.9 109.8 %all-reduce = f32[768,4]{0,1:T(4,128)S(1)} all-reduce(f32[768,4]{0,1:T(4,128)S(1)} %fusion.26), channel_id=3, replica_groups=mesh['req'=32,'tp'=8] {'req'}, use_global_device_ids=true, to_apply=%region_11.12.clone | all-reduce | flops 3072 | bytes 24576
  187.0 0.8 reshape.384
  187.8 0.4 fusion.25
  188.2 3.6 %fusion.37 = f32[24,4096]{1,0:T(8,128)} fusion(bf16[512,4096]{1,0:T(8,128)(2,1)} %param.25, bf16[3,8,4,128]{3,2,1,0:T(4,128)(2,1)S(1)} %bitcast.95), kind=kOutput, calls=%fused_computation.57 | convolution fusion | flops 100663296 | bytes 4612096 | tf_op jit(solution)/shard_map/dot_general | solution.py:190
  191.9 89.1 %all-reduce.3.cloned.1.call-done = f32[24,4096]{1,0:T(8,128)} async-done(((f32[24,4096]{1,0:T(8,128)}), f32[24,4096]{1,0:T(8,128)}) %all-reduce.3.cloned.1.call-update) | async-done | bytes 393232 | tf_op jit(solution)/shard_map/psum | solution.py:191
  281.0 1.2 multiply_reduce_fusion
  282.1 1.8 multiply_convert_fusion
  (181 shorter events, 9.2 us)
Async XLA Ops:
  7.2 68.7 %copy-start = (bf16[24,128,128]{2,1,0:T(8,128)(2,1)S(1)}, bf16[24,128,128]{2,1,0:T(8,128)(2,1)}, u32[]{:S(2)}) copy-start(bf16[24,128,128]{2,1,0:T(8,128)(2,1)} %param.20) | copy-start | bytes 2359300
  7.2 21.8 %copy-start.3 = (s32[2]{0:T(128)S(1)}, s32[2]{0:T(128)}, u32[]{:S(2)}) copy-start(s32[2]{0:T(128)} %param.23) | copy-start | bytes 28
  8.9 19.7 %all-to-all-start = ((bf16[32,24,512]{2,1,0:T(8,128)(2,1)}), bf16[32,24,512]{2,1,0:T(8,128)(2,1)S(1)}, u32[]{:S(2)}, u32[]{:S(2)}) async-start(bf16[32,24,512]{2,1,0:T(8,128)(2,1)} %tile.2), calls=%async_computation | async-start | bytes 1572864 | tf_op jit(solution)/shard_map/all_to_all | solution.py:129
  16.6 170.4 %reduce-scatter.3.cloned.1.call-start = ((), (), s32[]{:S(2)}) async-start(), calls=%async_computation.2 | async-start | bytes 1622016 | tf_op jit(solution)/shard_map/reduce_scatter | solution.py:143
  71.2 2.4 copy-start.2
  71.2 3.2 %copy-start.5 = (bf16[24,128]{1,0:T(8,128)(2,1)S(1)}, bf16[24,128]{1,0:T(8,128)(2,1)}, u32[]{:S(2)}) copy-start(bf16[24,128]{1,0:T(8,128)(2,1)} %param.17) | copy-start | bytes 18436
  71.2 3.2 %copy-start.8 = (u32[256]{0:T(256)S(1)}, u32[256]{0:T(256)}, u32[]{:S(2)}) copy-start(u32[256]{0:T(256)} %constant.130) | copy-start | bytes 3076
  71.2 4.5 %copy-start.7 = (bf16[24,128]{1,0:T(8,128)(2,1)S(1)}, bf16[24,128]{1,0:T(8,128)(2,1)}, u32[]{:S(2)}) copy-start(bf16[24,128]{1,0:T(8,128)(2,1)} %param.16) | copy-start | bytes 18436
  71.2 116.6 %copy-start.6 = (bf16[24,128,128]{2,1,0:T(8,128)(2,1)S(1)}, bf16[24,128,128]{2,1,0:T(8,128)(2,1)}, u32[]{:S(2)}) copy-start(bf16[24,128,128]{2,1,0:T(8,128)(2,1)} %param.21) | copy-start | bytes 2359300
  73.5 207.4 %all-reduce.3.cloned.1.call-start = ((), (), s32[]{:S(2)}) async-start(), calls=%async_computation.3 | async-start | bytes 786432 | tf_op jit(solution)/shard_map/psum | solution.py:191
  187.8 4.0 %copy-start.4 = (bf16[4096]{0:T(1024)(128)(2,1)S(1)}, bf16[4096]{0:T(1024)(128)(2,1)}, u32[]{:S(2)}) copy-start(bf16[4096]{0:T(1024)(128)(2,1)} %param.27) | copy-start | bytes 24580
  187.8 93.1 %copy-start.1 = (bf16[24,4096]{1,0:T(8,128)(2,1)S(1)}, bf16[24,4096]{1,0:T(8,128)(2,1)}, u32[]{:S(2)}) copy-start(bf16[24,4096]{1,0:T(8,128)(2,1)} %param.26) | copy-start | bytes 589828
Sparse Core Ops, SparseCore 0:
  73.6 87.0 reduce-scatter.2
  192.0 88.9 all-reduce.2
